TPU v7x, 32 devices: a whole 2x2x4 slice. The times are simulated.
32 devices in a mesh: section: 2 (over core), row: 4 (over y, x), col: 4 (over z).
Axes of the slice: x: 2, y: 2, z: 4, core: 2. Of those that a mesh axis runs over, the one named last changes fastest.
Arguments:
- checkpoints: bfloat16 [2, 4, 64, 128, 128], P('section', None, 'row', 'col'), may hold values from -1 to 1
- kernels: bfloat16 [4, 3, 3, 128, 128], P('section'), may hold values from -0.25 to 0.25
- cotangent: bfloat16 [4, 64, 128, 128], P(None, 'row', 'col'), may hold values from -1.5 to 1.5
- plan: int32 [4], replicated, may hold values from 0 to 3, each once
Outputs:
- boundary_grad: bfloat16 [2, 4, 64, 128, 128], P('section', None, 'row', 'col')
- kernel_grad: float32 [4, 3, 3, 128, 128], P('section')
Inputs may be any that keep to these rules, and one draw needn't show every extreme that they name: plan names each of the 4 microbatches exactly once; slot k of cotangent belongs to microbatch plan[k].
All inputs are finite; a program needn't handle non-finite values.
Results may differ from a plain program's by a relative error of at most 0.015.
Values may be sent and summed in bfloat16 or wider, within the bound.
No kernel may reach another device: no remote copies, remote signals or barrier semaphores. Data moves between devices by JAX's collectives and lax.ppermute only.
A program may use at most 64 MiB of HBM per device.

v0:
```python
import jax
import jax.numpy as jnp
from jax import lax
from jax.sharding import PartitionSpec as P


def extended(block, sides, width):
    for axis, dim in sides:
        count = lax.axis_size(axis)
        forward = [(i, i + 1) for i in range(count - 1)]
        backward = [(target, source) for source, target in forward]
        low = lax.ppermute(
            lax.slice_in_dim(block, block.shape[dim] - width, None, axis=dim), axis, forward
        )
        high = lax.ppermute(lax.slice_in_dim(block, 0, width, axis=dim), axis, backward)
        block = jnp.concatenate([low, block, high], axis=dim)
    return block


def passed_along(block, axis, distance):
    devices = range(lax.axis_size(axis))
    route = [(i - distance, i) for i in devices if i - distance in devices]
    return lax.ppermute(block, axis, route)


def convolve(padded, kernel):
    return lax.conv_general_dilated(
        padded,
        kernel,
        (1, 1),
        "VALID",
        dimension_numbers=("NHWC", "HWIO", "NHWC"),
        preferred_element_type=jnp.float32,
    )


def take_slots(values_in, slot_first, group_size):
    return lax.dynamic_slice_in_dim(values_in, slot_first, group_size, 0)


def kernel_terms(padded, signal):
    channels = signal.shape[3]
    flat_signal = signal.reshape(-1, channels)
    rows_out = []
    for a in range(3):
        tap_row = []
        for b in range(3):
            window = padded[:, a : a + signal.shape[1], b : b + signal.shape[2]].reshape(
                -1, channels
            )
            tap_row.append(
                lax.dot_general(
                    window,
                    flat_signal,
                    (((0,), (0,)), ((), ())),
                    preferred_element_type=jnp.float32,
                )
            )
        rows_out.append(jnp.stack(tap_row))
    return jnp.stack(rows_out)


def local(checkpoints, kernels, cotangent, plan):
    sections_count = lax.axis_size("section")
    section_index = lax.axis_index("section")
    batches = checkpoints.shape[1]
    tile_rows = checkpoints.shape[2]
    tile_cols = checkpoints.shape[3]
    channels = checkpoints.shape[4]
    layer_count = kernels.shape[0]
    flipped = jnp.transpose(kernels[:, ::-1, ::-1], (0, 1, 2, 4, 3))
    first_input = jnp.take(checkpoints[0], plan, axis=0)
    inputs_list = []
    outputs_list = []
    input_margin = []
    output_margin = []
    current = first_input
    for layer_idx in range(layer_count):
        padded = extended(current, (("row", 1), ("col", 2)), 1)
        inputs_list.append(padded)
        input_margin.append(1)
        current = jnp.tanh(convolve(padded, kernels[layer_idx])).astype(jnp.bfloat16)
        outputs_list.append(current)
        output_margin.append(0)
    groups = batches // batches
    tick_count = groups + sections_count - 1

    def backward(top_grad, slot_first):
        signals = [None] * layer_count
        gradient = top_grad.astype(jnp.float32)
        for layer_idx in reversed(range(layer_count)):
            output = take_slots(outputs_list[layer_idx], slot_first, batches).astype(jnp.float32)
            signal = (gradient * (1.0 - output * output)).astype(jnp.bfloat16)
            signals[layer_idx] = signal
            padded = extended(signal, (("row", 1), ("col", 2)), 1)
            gradient = convolve(padded, flipped[layer_idx])
        return (gradient.astype(jnp.bfloat16), signals)

    def tick_step(tick_idx, loop_state):
        incoming, boundary, gathered = loop_state
        slot_group = tick_idx - (sections_count - 1 - section_index)
        is_valid = (slot_group >= 0) & (slot_group < groups)
        slot_first = jnp.clip(slot_group, 0, groups - 1) * batches
        top_grad = jnp.where(section_index == sections_count - 1, cotangent, incoming)
        result, signals = backward(top_grad, slot_first)
        previous = boundary
        boundary = lax.dynamic_update_slice_in_dim(
            boundary, jnp.where(is_valid, result, previous), slot_first, 0
        )
        tap_terms = jnp.stack(
            [
                kernel_terms(
                    take_slots(inputs_list[layer_idx], slot_first, batches), signals[layer_idx]
                )
                for layer_idx in range(layer_count)
            ]
        )
        gathered = gathered + jnp.where(is_valid, tap_terms, 0.0)
        incoming = passed_along(result, "section", -1)
        return (incoming, boundary, gathered)

    incoming_zero = jnp.zeros((batches, tile_rows, tile_cols, channels), jnp.bfloat16)
    boundary_zero = jnp.zeros((batches, tile_rows, tile_cols, channels), jnp.bfloat16)
    gathered_zero = jnp.zeros((layer_count, 3, 3, channels, channels), jnp.float32)
    incoming, boundary, gathered = lax.fori_loop(
        0, tick_count, tick_step, (incoming_zero, boundary_zero, gathered_zero)
    )
    kernel_grad = (
        lax.psum(gathered.astype(jnp.bfloat16), ("row", "col")).astype(jnp.float32) / batches
    )
    boundary_grad = jnp.zeros_like(boundary).at[plan].set(boundary)[None]
    return (boundary_grad, kernel_grad)


def solution(mesh):
    return jax.shard_map(
        local,
        mesh=mesh,
        in_specs=(
            P("section", None, "row", "col", None),
            P("section", None, None, None, None),
            P(None, "row", "col", None),
            P(),
        ),
        out_specs=(P("section", None, "row", "col", None), P("section", None, None, None, None)),
        check_vma=False,
    )
```

profile of v0, /device:TPU:0, one launch (start us, length us, event | category | flops | bytes accessed | tf_op | source)
XLA Modules:
  0.0 291.0 jit_solution(17927654028252971086)
XLA Ops:
  9.5 1.3 collective-permute-start.10
  10.8 5.5 %collective-permute-start.9 = (bf16[4,1,32,128]{3,2,1,0:T(8,128)(2,1)S(1)}, bf16[4,1,32,128]{3,2,1,0:T(8,128)(2,1)S(1)}, u32[]{:S(2)}, u32[]{:S(2)}) collective-permute-start(bf16[4,1,32,128]{3,2,1,0:T(8,128)(2,1)S(1)} %get-tuple-element.383), channel_id=1, source_target_pairs={{0,4},{4,8},{8,12},{1,5},{5,9},{9,13},{2,6},{6,10},{10,14},{3,7},{... | collective-permute-start | bytes 98312 | tf_op jit(solution)/shard_map/ppermute | solution.py:12
  16.6 1.2 collective-permute-done.9
  18.5 4.0 %collective-permute-start.11 = (bf16[4,18,1,128]{3,2,1,0:T(2,128)(2,1)}, bf16[4,18,1,128]{3,2,1,0:T(2,128)(2,1)S(1)}, u32[]{:S(2)}, u32[]{:S(2)}) collective-permute-start(bf16[4,18,1,128]{3,2,1,0:T(2,128)(2,1)} %get-tuple-element.381), channel_id=1, source_target_pairs={{0,1},{1,2},{2,3},{4,5},{5,6},{6,7},{8,9},{9,10},{10,11},{12,13},{... | collective-permute-start | bytes 55304 | tf_op jit(solution)/shard_map/ppermute | solution.py:12
  22.5 1.3 collective-permute-start.12
  23.8 0.9 reverse_bitcast_fusion
  24.7 1.2 copy.94
  26.0 2.6 collective-permute-done.12
  30.2 1.7 fusion.39
  31.9 1.1 copy.85
  33.8 1.3 collective-permute-start.14
  35.1 4.9 %collective-permute-start.13 = (bf16[4,1,32,128]{3,2,0,1:T(8,128)(2,1)S(1)}, bf16[4,1,32,128]{3,2,0,1:T(8,128)(2,1)S(1)}, u32[]{:S(2)}, u32[]{:S(2)}) collective-permute-start(bf16[4,1,32,128]{3,2,0,1:T(8,128)(2,1)S(1)} %slice_bitcast_fusion.5), channel_id=1, source_target_pairs={{0,4},{4,8},{8,12},{1,5},{5,9},{9,13},{2,6},{6,10},{10,14},{3,7},{... | collective-permute-start | bytes 98312 | tf_op jit(solution)/shard_map/ppermute | solution.py:12
  40.1 1.1 slice_bitcast_fusion.3
  41.7 3.5 %collective-permute-start.15 = (bf16[4,18,1,128]{3,1,2,0:T(8,128)(2,1)S(1)}, bf16[4,18,1,128]{3,1,2,0:T(8,128)(2,1)S(1)}, u32[]{:S(2)}, u32[]{:S(2)}) collective-permute-start(bf16[4,18,1,128]{3,1,2,0:T(8,128)(2,1)S(1)} %get-tuple-element.377), channel_id=1, source_target_pairs={{0,1},{1,2},{2,3},{4,5},{5,6},{6,7},{8,9},{9,10},{10,11},{12,13},{... | collective-permute-start | bytes 55304 | tf_op jit(solution)/shard_map/ppermute | solution.py:12
  45.2 1.3 collective-permute-start.16
  46.9 1.0 copy.95
  48.0 3.0 %collective-permute-done.16 = bf16[4,18,1,128]{3,1,2,0:T(8,128)(2,1)S(1)} collective-permute-done((bf16[4,18,1,128]{3,1,2,0:T(8,128)(2,1)S(1)}, bf16[4,18,1,128]{3,1,2,0:T(8,128)(2,1)S(1)}, u32[]{:S(2)}, u32[]{:S(2)}) %collective-permute-start.16) | collective-permute-done | bytes 18464 | tf_op jit(solution)/shard_map/ppermute | solution.py:15
  50.9 1.4 pad_maximum_fusion.6
  53.9 1.7 fusion.38
  55.9 0.8 slice_bitcast_fusion.2
  56.7 0.9 broadcast.30.clone.1
  57.6 106.7 %while.20 = (s32[]{:T(128)}, bf16[4,16,32,128]{3,1,2,0:T(8,128)(2,1)}, bf16[4,16,32,128]{3,1,2,0:T(8,128)(2,1)}, f32[2,3,3,128,128]{3,4,2,1,0:T(8,128)S(1)}, pre...) while((s32[]{:T(128)}, ...), condition=%wide.region_1.2_spmd.clone, body=%wide.region_0.1_spmd.clone.sunk | while | flops 2737602560 | bytes 72510144 | solution.py:125
  57.6 1.7 multiply_convert_fusion.2
  59.4 1.3 collective-permute-start
  60.7 5.8 %collective-permute-start.1 = (bf16[4,1,32,128]{3,1,2,0:T(2,128)(2,1)S(1)}, bf16[4,1,32,128]{3,1,2,0:T(2,128)(2,1)S(1)}, u32[]{:S(2)}, u32[]{:S(2)}) collective-permute-start(bf16[4,1,32,128]{3,1,2,0:T(2,128)(2,1)S(1)} %get-tuple-element.471), channel_id=1, source_target_pairs={{0,4},{4,8},{8,12},{1,5},{5,9},{9,13},{2,6},{6,10},{10,14},{3,7},{... | collective-permute-start | bytes 98312 | tf_op jit(solution)/shard_map/while/body/eval_jaxpr/ppermute | solution.py:12
  69.7 1.3 collective-permute-start.2
  71.0 5.2 %collective-permute-start.3 = (bf16[4,18,1,128]{3,1,2,0:T(8,128)(2,1)S(1)}, bf16[4,18,1,128]{3,1,2,0:T(8,128)(2,1)}, u32[]{:S(2)}, u32[]{:S(2)}) collective-permute-start(bf16[4,18,1,128]{3,1,2,0:T(8,128)(2,1)S(1)} %get-tuple-element.473), channel_id=1, source_target_pairs={{0,1},{1,2},{2,3},{4,5},{5,6},{6,7},{8,9},{9,10},{10,11},{12,13},{... | collective-permute-start | bytes 55304 | tf_op jit(solution)/shard_map/while/body/eval_jaxpr/ppermute | solution.py:12
  76.2 0.8 collective-permute-done.3
  77.0 1.2 maximum_bitcast_fusion.18
  79.8 1.7 convolution_select_fusion.5
  82.5 1.0 copy-done.5
  86.7 1.3 collective-permute-start.4
  88.0 5.7 %collective-permute-start.5 = (bf16[4,1,32,128]{3,1,2,0:T(2,128)(2,1)S(1)}, bf16[4,1,32,128]{3,1,2,0:T(2,128)(2,1)S(1)}, u32[]{:S(2)}, u32[]{:S(2)}) collective-permute-start(bf16[4,1,32,128]{3,1,2,0:T(2,128)(2,1)S(1)} %get-tuple-element.475), channel_id=1, source_target_pairs={{0,4},{4,8},{8,12},{1,5},{5,9},{9,13},{2,6},{6,10},{10,14},{3,7},{... | collective-permute-start | bytes 98312 | tf_op jit(solution)/shard_map/while/body/eval_jaxpr/ppermute | solution.py:12
  94.0 1.6 collective-permute-done.5
  95.6 1.3 collective-permute-start.6
  96.9 4.9 %collective-permute-start.7 = (bf16[4,18,1,128]{3,1,2,0:T(8,128)(2,1)S(1)}, bf16[4,18,1,128]{3,1,2,0:T(8,128)(2,1)S(1)}, u32[]{:S(2)}, u32[]{:S(2)}) collective-permute-start(bf16[4,18,1,128]{3,1,2,0:T(8,128)(2,1)S(1)} %get-tuple-element.477), channel_id=1, source_target_pairs={{0,1},{1,2},{2,3},{4,5},{5,6},{6,7},{8,9},{9,10},{10,11},{12,13},{... | collective-permute-start | bytes 55304 | tf_op jit(solution)/shard_map/while/body/eval_jaxpr/ppermute | solution.py:12
  102.0 1.4 collective-permute-done.7
  104.9 1.7 fusion.166
  107.0 1.3 collective-permute-start.8
  108.7 0.9 select_select_fusion.2
  109.5 1.3 collective-permute-done.8
  110.9 1.7 multiply_convert_fusion.2
  112.7 1.3 collective-permute-start
  114.0 5.4 %collective-permute-start.1 = (bf16[4,1,32,128]{3,1,2,0:T(2,128)(2,1)S(1)}, bf16[4,1,32,128]{3,1,2,0:T(2,128)(2,1)S(1)}, u32[]{:S(2)}, u32[]{:S(2)}) collective-permute-start(bf16[4,1,32,128]{3,1,2,0:T(2,128)(2,1)S(1)} %get-tuple-element.471), channel_id=1, source_target_pairs={{0,4},{4,8},{8,12},{1,5},{5,9},{9,13},{2,6},{6,10},{10,14},{3,7},{... | collective-permute-start | bytes 98312 | tf_op jit(solution)/shard_map/while/body/eval_jaxpr/ppermute | solution.py:12
  122.7 1.3 collective-permute-start.2
  124.0 5.5 %collective-permute-start.3 = (bf16[4,18,1,128]{3,1,2,0:T(8,128)(2,1)S(1)}, bf16[4,18,1,128]{3,1,2,0:T(8,128)(2,1)}, u32[]{:S(2)}, u32[]{:S(2)}) collective-permute-start(bf16[4,18,1,128]{3,1,2,0:T(8,128)(2,1)S(1)} %get-tuple-element.473), channel_id=1, source_target_pairs={{0,1},{1,2},{2,3},{4,5},{5,6},{6,7},{8,9},{9,10},{10,11},{12,13},{... | collective-permute-start | bytes 55304 | tf_op jit(solution)/shard_map/while/body/eval_jaxpr/ppermute | solution.py:12
  129.5 0.8 collective-permute-done.3
  130.4 1.2 maximum_bitcast_fusion.18
  133.1 1.7 convolution_select_fusion.5
  135.8 1.0 copy-done.5
  140.0 1.3 collective-permute-start.4
  141.3 5.8 %collective-permute-start.5 = (bf16[4,1,32,128]{3,1,2,0:T(2,128)(2,1)S(1)}, bf16[4,1,32,128]{3,1,2,0:T(2,128)(2,1)S(1)}, u32[]{:S(2)}, u32[]{:S(2)}) collective-permute-start(bf16[4,1,32,128]{3,1,2,0:T(2,128)(2,1)S(1)} %get-tuple-element.475), channel_id=1, source_target_pairs={{0,4},{4,8},{8,12},{1,5},{5,9},{9,13},{2,6},{6,10},{10,14},{3,7},{... | collective-permute-start | bytes 98312 | tf_op jit(solution)/shard_map/while/body/eval_jaxpr/ppermute | solution.py:12
  147.4 1.6 collective-permute-done.5
  149.0 1.3 collective-permute-start.6
  150.3 4.9 %collective-permute-start.7 = (bf16[4,18,1,128]{3,1,2,0:T(8,128)(2,1)S(1)}, bf16[4,18,1,128]{3,1,2,0:T(8,128)(2,1)S(1)}, u32[]{:S(2)}, u32[]{:S(2)}) collective-permute-start(bf16[4,18,1,128]{3,1,2,0:T(8,128)(2,1)S(1)} %get-tuple-element.477), channel_id=1, source_target_pairs={{0,1},{1,2},{2,3},{4,5},{5,6},{6,7},{8,9},{9,10},{10,11},{12,13},{... | collective-permute-start | bytes 55304 | tf_op jit(solution)/shard_map/while/body/eval_jaxpr/ppermute | solution.py:12
  155.3 1.4 collective-permute-done.7
  158.3 1.7 fusion.166
  160.3 1.3 collective-permute-start.8
  162.0 2.0 select_select_fusion.2
  164.2 1.1 copy.97
  165.3 1.2 copy.96
  166.6 0.8 scatter_fusion
  167.4 114.6 %all-reduce.2.cloned.1.call-done = bf16[2,3,3,128,128]{4,3,2,1,0:T(8,128)(2,1)} async-done(((bf16[2,3,3,128,128]{4,3,2,1,0:T(8,128)(2,1)}), bf16[2,3,3,128,128]{4,3,2,1,0:T(8,128)(2,1)}) %all-reduce.2.cloned.1.call-update) | async-done | bytes 589840 | tf_op jit(solution)/shard_map/psum | solution.py:129
  282.0 2.2 convert_multiply_fusion
  (166 shorter events, 31.7 us)
Async XLA Ops:
  7.2 1.5 copy-start
  7.2 9.1 %copy-start.6 = (bf16[2,3,3,128,128]{4,3,2,1,0:T(8,128)(2,1)S(1)}, bf16[2,3,3,128,128]{4,3,2,1,0:T(8,128)(2,1)}, u32[]{:S(2)}) copy-start(bf16[2,3,3,128,128]{4,3,2,1,0:T(8,128)(2,1)} %param.7) | copy-start | bytes 1769476
  7.2 274.8 %all-reduce.2.cloned.1.call-start = ((), (), s32[]{:S(2)}) async-start(), calls=%async_computation | async-start | bytes 1179648 | tf_op jit(solution)/shard_map/psum | solution.py:129
  8.0 0.7 copy-start.9
  9.5 7.1 %collective-permute-start.10 = (bf16[4,1,32,128]{3,2,1,0:T(8,128)(2,1)S(1)}, bf16[4,1,32,128]{3,2,1,0:T(8,128)(2,1)S(1)}, u32[]{:S(2)}, u32[]{:S(2)}) collective-permute-start(bf16[4,1,32,128]{3,2,1,0:T(8,128)(2,1)S(1)} %get-tuple-element.384), channel_id=1, source_target_pairs={{4,0},{8,4},{12,8},{5,1},{9,5},{13,9},{6,2},{10,6},{14,10},{7,3},{... | collective-permute-start | bytes 98312 | tf_op jit(solution)/shard_map/ppermute | solution.py:15
  10.8 7.1 %collective-permute-start.9 = (bf16[4,1,32,128]{3,2,1,0:T(8,128)(2,1)S(1)}, bf16[4,1,32,128]{3,2,1,0:T(8,128)(2,1)S(1)}, u32[]{:S(2)}, u32[]{:S(2)}) collective-permute-start(bf16[4,1,32,128]{3,2,1,0:T(8,128)(2,1)S(1)} %get-tuple-element.383), channel_id=1, source_target_pairs={{0,4},{4,8},{8,12},{1,5},{5,9},{9,13},{2,6},{6,10},{10,14},{3,7},{... | collective-permute-start | bytes 98312 | tf_op jit(solution)/shard_map/ppermute | solution.py:12
  18.5 7.5 %collective-permute-start.11 = (bf16[4,18,1,128]{3,2,1,0:T(2,128)(2,1)}, bf16[4,18,1,128]{3,2,1,0:T(2,128)(2,1)S(1)}, u32[]{:S(2)}, u32[]{:S(2)}) collective-permute-start(bf16[4,18,1,128]{3,2,1,0:T(2,128)(2,1)} %get-tuple-element.381), channel_id=1, source_target_pairs={{0,1},{1,2},{2,3},{4,5},{5,6},{6,7},{8,9},{9,10},{10,11},{12,13},{... | collective-permute-start | bytes 55304 | tf_op jit(solution)/shard_map/ppermute | solution.py:12
  22.5 6.1 %collective-permute-start.12 = (bf16[4,18,1,128]{3,2,1,0:T(2,128)(2,1)}, bf16[4,18,1,128]{3,2,1,0:T(2,128)(2,1)S(1)}, u32[]{:S(2)}, u32[]{:S(2)}) collective-permute-start(bf16[4,18,1,128]{3,2,1,0:T(2,128)(2,1)} %get-tuple-element.382), channel_id=1, source_target_pairs={{1,0},{2,1},{3,2},{5,4},{6,5},{7,6},{9,8},{10,9},{11,10},{13,12},{... | collective-permute-start | bytes 55304 | tf_op jit(solution)/shard_map/ppermute | solution.py:15
  29.5 0.7 copy-start.11
  33.8 7.9 %collective-permute-start.14 = (bf16[4,1,32,128]{3,1,2,0:T(2,128)(2,1)}, bf16[4,1,32,128]{3,1,2,0:T(2,128)(2,1)S(1)}, u32[]{:S(2)}, u32[]{:S(2)}) collective-permute-start(bf16[4,1,32,128]{3,1,2,0:T(2,128)(2,1)} %copy.87), channel_id=1, source_target_pairs={{4,0},{8,4},{12,8},{5,1},{9,5},{13,9},{6,2},{10,6},{14,10},{7,3},{... | collective-permute-start | bytes 98312 | tf_op jit(solution)/shard_map/ppermute | solution.py:15
  35.1 6.5 %collective-permute-start.13 = (bf16[4,1,32,128]{3,2,0,1:T(8,128)(2,1)S(1)}, bf16[4,1,32,128]{3,2,0,1:T(8,128)(2,1)S(1)}, u32[]{:S(2)}, u32[]{:S(2)}) collective-permute-start(bf16[4,1,32,128]{3,2,0,1:T(8,128)(2,1)S(1)} %slice_bitcast_fusion.5), channel_id=1, source_target_pairs={{0,4},{4,8},{8,12},{1,5},{5,9},{9,13},{2,6},{6,10},{10,14},{3,7},{... | collective-permute-start | bytes 98312 | tf_op jit(solution)/shard_map/ppermute | solution.py:12
  41.7 6.2 %collective-permute-start.15 = (bf16[4,18,1,128]{3,1,2,0:T(8,128)(2,1)S(1)}, bf16[4,18,1,128]{3,1,2,0:T(8,128)(2,1)S(1)}, u32[]{:S(2)}, u32[]{:S(2)}) collective-permute-start(bf16[4,18,1,128]{3,1,2,0:T(8,128)(2,1)S(1)} %get-tuple-element.377), channel_id=1, source_target_pairs={{0,1},{1,2},{2,3},{4,5},{5,6},{6,7},{8,9},{9,10},{10,11},{12,13},{... | collective-permute-start | bytes 55304 | tf_op jit(solution)/shard_map/ppermute | solution.py:12
  45.2 5.7 %collective-permute-start.16 = (bf16[4,18,1,128]{3,1,2,0:T(8,128)(2,1)S(1)}, bf16[4,18,1,128]{3,1,2,0:T(8,128)(2,1)S(1)}, u32[]{:S(2)}, u32[]{:S(2)}) collective-permute-start(bf16[4,18,1,128]{3,1,2,0:T(8,128)(2,1)S(1)} %get-tuple-element.378), channel_id=1, source_target_pairs={{1,0},{2,1},{3,2},{5,4},{6,5},{7,6},{9,8},{10,9},{11,10},{13,12},{... | collective-permute-start | bytes 55304 | tf_op jit(solution)/shard_map/ppermute | solution.py:15
  52.8 1.1 copy-start.7
  57.6 9.2 %copy-start.1 = (bf16[4,16,32,128]{3,1,2,0:T(8,128)(2,1)}, bf16[4,16,32,128]{3,1,2,0:T(8,128)(2,1)S(1)}, u32[]{:S(2)}) copy-start(bf16[4,16,32,128]{3,1,2,0:T(8,128)(2,1)S(1)} %get-tuple-element.519) | copy-start | bytes 1572868 | tf_op jit(solution)/shard_map/while
  57.6 8.9 %copy-start.4 = (bf16[4,18,34,128]{3,1,2,0:T(8,128)(2,1)S(1)}, bf16[4,18,34,128]{3,1,2,0:T(8,128)(2,1)}, u32[]{:S(2)}) copy-start(bf16[4,18,34,128]{3,1,2,0:T(8,128)(2,1)} %get-tuple-element.525) | copy-start | bytes 1880068 | tf_op jit(solution)/shard_map/while
  59.4 10.2 %collective-permute-start = (bf16[4,1,32,128]{3,1,2,0:T(2,128)(2,1)S(1)}, bf16[4,1,32,128]{3,1,2,0:T(2,128)(2,1)S(1)}, u32[]{:S(2)}, u32[]{:S(2)}) collective-permute-start(bf16[4,1,32,128]{3,1,2,0:T(2,128)(2,1)S(1)} %get-tuple-element.470), channel_id=1, source_target_pairs={{4,0},{8,4},{12,8},{5,1},{9,5},{13,9},{6,2},{10,6},{14,10},{7,3},{... | collective-permute-start | bytes 98312 | tf_op jit(solution)/shard_map/while/body/eval_jaxpr/ppermute | solution.py:15
  60.7 8.9 %collective-permute-start.1 = (bf16[4,1,32,128]{3,1,2,0:T(2,128)(2,1)S(1)}, bf16[4,1,32,128]{3,1,2,0:T(2,128)(2,1)S(1)}, u32[]{:S(2)}, u32[]{:S(2)}) collective-permute-start(bf16[4,1,32,128]{3,1,2,0:T(2,128)(2,1)S(1)} %get-tuple-element.471), channel_id=1, source_target_pairs={{0,4},{4,8},{8,12},{1,5},{5,9},{9,13},{2,6},{6,10},{10,14},{3,7},{... | collective-permute-start | bytes 98312 | tf_op jit(solution)/shard_map/while/body/eval_jaxpr/ppermute | solution.py:12
  69.7 6.5 %collective-permute-start.2 = (bf16[4,18,1,128]{3,1,2,0:T(8,128)(2,1)S(1)}, bf16[4,18,1,128]{3,1,2,0:T(8,128)(2,1)S(1)}, u32[]{:S(2)}, u32[]{:S(2)}) collective-permute-start(bf16[4,18,1,128]{3,1,2,0:T(8,128)(2,1)S(1)} %get-tuple-element.472), channel_id=1, source_target_pairs={{1,0},{2,1},{3,2},{5,4},{6,5},{7,6},{9,8},{10,9},{11,10},{13,12},{... | collective-permute-start | bytes 55304 | tf_op jit(solution)/shard_map/while/body/eval_jaxpr/ppermute | solution.py:15
  71.0 6.1 %collective-permute-start.3 = (bf16[4,18,1,128]{3,1,2,0:T(8,128)(2,1)S(1)}, bf16[4,18,1,128]{3,1,2,0:T(8,128)(2,1)}, u32[]{:S(2)}, u32[]{:S(2)}) collective-permute-start(bf16[4,18,1,128]{3,1,2,0:T(8,128)(2,1)S(1)} %get-tuple-element.473), channel_id=1, source_target_pairs={{0,1},{1,2},{2,3},{4,5},{5,6},{6,7},{8,9},{9,10},{10,11},{12,13},{... | collective-permute-start | bytes 55304 | tf_op jit(solution)/shard_map/while/body/eval_jaxpr/ppermute | solution.py:12
  78.8 1.1 copy-start.8
  82.3 1.2 copy-start.5
  86.7 7.4 %collective-permute-start.4 = (bf16[4,1,32,128]{3,1,2,0:T(2,128)(2,1)S(1)}, bf16[4,1,32,128]{3,1,2,0:T(2,128)(2,1)S(1)}, u32[]{:S(2)}, u32[]{:S(2)}) collective-permute-start(bf16[4,1,32,128]{3,1,2,0:T(2,128)(2,1)S(1)} %get-tuple-element.474), channel_id=1, source_target_pairs={{4,0},{8,4},{12,8},{5,1},{9,5},{13,9},{6,2},{10,6},{14,10},{7,3},{... | collective-permute-start | bytes 98312 | tf_op jit(solution)/shard_map/while/body/eval_jaxpr/ppermute | solution.py:15
  88.0 7.6 %collective-permute-start.5 = (bf16[4,1,32,128]{3,1,2,0:T(2,128)(2,1)S(1)}, bf16[4,1,32,128]{3,1,2,0:T(2,128)(2,1)S(1)}, u32[]{:S(2)}, u32[]{:S(2)}) collective-permute-start(bf16[4,1,32,128]{3,1,2,0:T(2,128)(2,1)S(1)} %get-tuple-element.475), channel_id=1, source_target_pairs={{0,4},{4,8},{8,12},{1,5},{5,9},{9,13},{2,6},{6,10},{10,14},{3,7},{... | collective-permute-start | bytes 98312 | tf_op jit(solution)/shard_map/while/body/eval_jaxpr/ppermute | solution.py:12
  95.6 6.3 %collective-permute-start.6 = (bf16[4,18,1,128]{3,1,2,0:T(8,128)(2,1)S(1)}, bf16[4,18,1,128]{3,1,2,0:T(8,128)(2,1)S(1)}, u32[]{:S(2)}, u32[]{:S(2)}) collective-permute-start(bf16[4,18,1,128]{3,1,2,0:T(8,128)(2,1)S(1)} %get-tuple-element.476), channel_id=1, source_target_pairs={{1,0},{2,1},{3,2},{5,4},{6,5},{7,6},{9,8},{10,9},{11,10},{13,12},{... | collective-permute-start | bytes 55304 | tf_op jit(solution)/shard_map/while/body/eval_jaxpr/ppermute | solution.py:15
  96.9 6.5 %collective-permute-start.7 = (bf16[4,18,1,128]{3,1,2,0:T(8,128)(2,1)S(1)}, bf16[4,18,1,128]{3,1,2,0:T(8,128)(2,1)S(1)}, u32[]{:S(2)}, u32[]{:S(2)}) collective-permute-start(bf16[4,18,1,128]{3,1,2,0:T(8,128)(2,1)S(1)} %get-tuple-element.477), channel_id=1, source_target_pairs={{0,1},{1,2},{2,3},{4,5},{5,6},{6,7},{8,9},{9,10},{10,11},{12,13},{... | collective-permute-start | bytes 55304 | tf_op jit(solution)/shard_map/while/body/eval_jaxpr/ppermute | solution.py:12
  107.0 3.9 %collective-permute-start.8 = (bf16[4,16,32,128]{3,1,2,0:T(8,128)(2,1)S(1)}, bf16[4,16,32,128]{3,1,2,0:T(8,128)(2,1)}, u32[]{:S(2)}, u32[]{:S(2)}) collective-permute-start(bf16[4,16,32,128]{3,1,2,0:T(8,128)(2,1)S(1)} %slice_bitcast_fusion.7), channel_id=1, source_target_pairs={{16,0},{17,1},{18,2},{19,3},{20,4},{21,5},{22,6},{23,7},{24,8},{25... | collective-permute-start | bytes 1572872 | tf_op jit(solution)/shard_map/while/body/eval_jaxpr/ppermute | solution.py:23
  108.7 2.2 copy-start.2
  110.9 8.9 %copy-start.1 = (bf16[4,16,32,128]{3,1,2,0:T(8,128)(2,1)}, bf16[4,16,32,128]{3,1,2,0:T(8,128)(2,1)S(1)}, u32[]{:S(2)}) copy-start(bf16[4,16,32,128]{3,1,2,0:T(8,128)(2,1)S(1)} %get-tuple-element.519) | copy-start | bytes 1572868 | tf_op jit(solution)/shard_map/while
  110.9 8.6 %copy-start.4 = (bf16[4,18,34,128]{3,1,2,0:T(8,128)(2,1)S(1)}, bf16[4,18,34,128]{3,1,2,0:T(8,128)(2,1)}, u32[]{:S(2)}) copy-start(bf16[4,18,34,128]{3,1,2,0:T(8,128)(2,1)} %get-tuple-element.525) | copy-start | bytes 1880068 | tf_op jit(solution)/shard_map/while
  112.7 9.9 %collective-permute-start = (bf16[4,1,32,128]{3,1,2,0:T(2,128)(2,1)S(1)}, bf16[4,1,32,128]{3,1,2,0:T(2,128)(2,1)S(1)}, u32[]{:S(2)}, u32[]{:S(2)}) collective-permute-start(bf16[4,1,32,128]{3,1,2,0:T(2,128)(2,1)S(1)} %get-tuple-element.470), channel_id=1, source_target_pairs={{4,0},{8,4},{12,8},{5,1},{9,5},{13,9},{6,2},{10,6},{14,10},{7,3},{... | collective-permute-start | bytes 98312 | tf_op jit(solution)/shard_map/while/body/eval_jaxpr/ppermute | solution.py:15
  114.0 8.6 %collective-permute-start.1 = (bf16[4,1,32,128]{3,1,2,0:T(2,128)(2,1)S(1)}, bf16[4,1,32,128]{3,1,2,0:T(2,128)(2,1)S(1)}, u32[]{:S(2)}, u32[]{:S(2)}) collective-permute-start(bf16[4,1,32,128]{3,1,2,0:T(2,128)(2,1)S(1)} %get-tuple-element.471), channel_id=1, source_target_pairs={{0,4},{4,8},{8,12},{1,5},{5,9},{9,13},{2,6},{6,10},{10,14},{3,7},{... | collective-permute-start | bytes 98312 | tf_op jit(solution)/shard_map/while/body/eval_jaxpr/ppermute | solution.py:12
  122.7 6.8 %collective-permute-start.2 = (bf16[4,18,1,128]{3,1,2,0:T(8,128)(2,1)S(1)}, bf16[4,18,1,128]{3,1,2,0:T(8,128)(2,1)S(1)}, u32[]{:S(2)}, u32[]{:S(2)}) collective-permute-start(bf16[4,18,1,128]{3,1,2,0:T(8,128)(2,1)S(1)} %get-tuple-element.472), channel_id=1, source_target_pairs={{1,0},{2,1},{3,2},{5,4},{6,5},{7,6},{9,8},{10,9},{11,10},{13,12},{... | collective-permute-start | bytes 55304 | tf_op jit(solution)/shard_map/while/body/eval_jaxpr/ppermute | solution.py:15
  124.0 6.4 %collective-permute-start.3 = (bf16[4,18,1,128]{3,1,2,0:T(8,128)(2,1)S(1)}, bf16[4,18,1,128]{3,1,2,0:T(8,128)(2,1)}, u32[]{:S(2)}, u32[]{:S(2)}) collective-permute-start(bf16[4,18,1,128]{3,1,2,0:T(8,128)(2,1)S(1)} %get-tuple-element.473), channel_id=1, source_target_pairs={{0,1},{1,2},{2,3},{4,5},{5,6},{6,7},{8,9},{9,10},{10,11},{12,13},{... | collective-permute-start | bytes 55304 | tf_op jit(solution)/shard_map/while/body/eval_jaxpr/ppermute | solution.py:12
  132.1 1.1 copy-start.8
  135.6 1.2 copy-start.5
  140.0 7.4 %collective-permute-start.4 = (bf16[4,1,32,128]{3,1,2,0:T(2,128)(2,1)S(1)}, bf16[4,1,32,128]{3,1,2,0:T(2,128)(2,1)S(1)}, u32[]{:S(2)}, u32[]{:S(2)}) collective-permute-start(bf16[4,1,32,128]{3,1,2,0:T(2,128)(2,1)S(1)} %get-tuple-element.474), channel_id=1, source_target_pairs={{4,0},{8,4},{12,8},{5,1},{9,5},{13,9},{6,2},{10,6},{14,10},{7,3},{... | collective-permute-start | bytes 98312 | tf_op jit(solution)/shard_map/while/body/eval_jaxpr/ppermute | solution.py:15
  141.3 7.7 %collective-permute-start.5 = (bf16[4,1,32,128]{3,1,2,0:T(2,128)(2,1)S(1)}, bf16[4,1,32,128]{3,1,2,0:T(2,128)(2,1)S(1)}, u32[]{:S(2)}, u32[]{:S(2)}) collective-permute-start(bf16[4,1,32,128]{3,1,2,0:T(2,128)(2,1)S(1)} %get-tuple-element.475), channel_id=1, source_target_pairs={{0,4},{4,8},{8,12},{1,5},{5,9},{9,13},{2,6},{6,10},{10,14},{3,7},{... | collective-permute-start | bytes 98312 | tf_op jit(solution)/shard_map/while/body/eval_jaxpr/ppermute | solution.py:12
  149.0 6.3 %collective-permute-start.6 = (bf16[4,18,1,128]{3,1,2,0:T(8,128)(2,1)S(1)}, bf16[4,18,1,128]{3,1,2,0:T(8,128)(2,1)S(1)}, u32[]{:S(2)}, u32[]{:S(2)}) collective-permute-start(bf16[4,18,1,128]{3,1,2,0:T(8,128)(2,1)S(1)} %get-tuple-element.476), channel_id=1, source_target_pairs={{1,0},{2,1},{3,2},{5,4},{6,5},{7,6},{9,8},{10,9},{11,10},{13,12},{... | collective-permute-start | bytes 55304 | tf_op jit(solution)/shard_map/while/body/eval_jaxpr/ppermute | solution.py:15
  150.3 6.5 %collective-permute-start.7 = (bf16[4,18,1,128]{3,1,2,0:T(8,128)(2,1)S(1)}, bf16[4,18,1,128]{3,1,2,0:T(8,128)(2,1)S(1)}, u32[]{:S(2)}, u32[]{:S(2)}) collective-permute-start(bf16[4,18,1,128]{3,1,2,0:T(8,128)(2,1)S(1)} %get-tuple-element.477), channel_id=1, source_target_pairs={{0,1},{1,2},{2,3},{4,5},{5,6},{6,7},{8,9},{9,10},{10,11},{12,13},{... | collective-permute-start | bytes 55304 | tf_op jit(solution)/shard_map/while/body/eval_jaxpr/ppermute | solution.py:12
  160.3 3.9 %collective-permute-start.8 = (bf16[4,16,32,128]{3,1,2,0:T(8,128)(2,1)S(1)}, bf16[4,16,32,128]{3,1,2,0:T(8,128)(2,1)}, u32[]{:S(2)}, u32[]{:S(2)}) collective-permute-start(bf16[4,16,32,128]{3,1,2,0:T(8,128)(2,1)S(1)} %slice_bitcast_fusion.7), channel_id=1, source_target_pairs={{16,0},{17,1},{18,2},{19,3},{20,4},{21,5},{22,6},{23,7},{24,8},{25... | collective-permute-start | bytes 1572872 | tf_op jit(solution)/shard_map/while/body/eval_jaxpr/ppermute | solution.py:23
  162.0 2.2 copy-start.2
  165.3 1.3 copy-start.10
  167.4 116.8 %copy-start.3 = (bf16[4,16,32,128]{3,2,1,0:T(8,128)(2,1)}, bf16[4,16,32,128]{3,2,1,0:T(8,128)(2,1)S(1)}, u32[]{:S(2)}) copy-start(bf16[4,16,32,128]{3,2,1,0:T(8,128)(2,1)S(1)} %scatter_fusion) | copy-start | bytes 1572868
Sparse Core Ops, SparseCore 0:
  165.4 116.5 all-reduce.1
where the time goes:
time: 293 us; the launch traced here: 291 us
  waiting for transfers between devices  132 us (45%)
  starting transfers between devices  79.3 us (27%)
  matrix products  22.4 us (8%)
  local copies, waits for them, and re-layouts  21.9 us (7%)
  other arithmetic  20.5 us (7%)
  between operations  14.4 us (5%)
    psum x1, waiting for transfers between devices, local(): lax.psum(gathered.astype(jnp.bfloat16), ('row', 'col')).astype(jnp.float32)  115 us
    ppermute x12, starting transfers between devices, extended(): lax.ppermute(lax.slice_in_dim(block, block.shape[dim] - width, None, axis...  61.2 us
    ppermute x12, starting transfers between devices, extended(): lax.ppermute(lax.slice_in_dim(block, 0, width, axis=dim), axis, backward)  15.5 us
    dot_general x36, matrix products, kernel_terms(): lax.dot_general(window, flat_signal, (((0,), (0,)), ((), ())), preferred_...  12.2 us
    conv_general_dilated x6, matrix products, convolve(): lax.conv_general_dilated(padded, kernel, (1, 1), 'VALID', dimension_numbe...  10.2 us
    ppermute x12, waiting for transfers between devices, extended(): lax.ppermute(lax.slice_in_dim(block, block.shape[dim] - width, None, axis...  9.45 us
    ppermute x12, waiting for transfers between devices, extended(): lax.ppermute(lax.slice_in_dim(block, 0, width, axis=dim), axis, backward)  6.07 us
  transfers between devices with their start and end apart: 27, of which 15 were waited for; matrix products, arithmetic and copies ran while one was open for 6% of the time, Pallas kernels for 0%

commit v1 on v0

--- a/solution.py
+++ b/solution.py
@@ -126,7 +126,10 @@
         0, tick_count, tick_step, (incoming_zero, boundary_zero, gathered_zero)
     )
     kernel_grad = (
-        lax.psum(gathered.astype(jnp.bfloat16), ("row", "col")).astype(jnp.float32) / batches
+        jnp.sum(lax.all_gather(gathered.astype(jnp.bfloat16), ("row", "col")), axis=0).astype(
+            jnp.float32
+        )
+        / batches
     )
     boundary_grad = jnp.zeros_like(boundary).at[plan].set(boundary)[None]
     return (boundary_grad, kernel_grad)

time: 293 us -> 312 us (1.065)
  waiting for transfers between devices: 132 us -> 149 us
  starting transfers between devices: 79.3 us -> 75.5 us
  other arithmetic: 20.5 us -> 24.2 us
    all_gather x0 -> x1, waiting for transfers between devices: none -> 126 us  [local(): lax.all_gather(gathered.astype(jnp.bfloat16), ('row', 'col'))]
    psum x1 -> x0, waiting for transfers between devices: 115 us -> none  [local(): lax.psum(gathered.astype(jnp.bfloat16), ('row', 'col')).astype(jnp.float32)]
    ppermute x12, waiting for transfers between devices: 6.07 us -> 13.2 us  [extended(): lax.ppermute(lax.slice_in_dim(block, 0, width, axis=dim), axis, backward)]
    reduce_sum x0 -> x1, other arithmetic: none -> 5.82 us  [local(): jnp.sum(lax.all_gather(gathered.astype(jnp.bfloat16), ('row', 'col')), ax...]
    ppermute x12, starting transfers between devices: 61.2 us -> 57.3 us  [extended(): lax.ppermute(lax.slice_in_dim(block, block.shape[dim] - width, None, axis...]
where the time goes in v1:
time: 312 us; the launch traced here: 310 us
  waiting for transfers between devices  149 us (48%)
  starting transfers between devices  75.5 us (24%)
  local copies, waits for them, and re-layouts  24.4 us (8%)
  other arithmetic  24.2 us (8%)
  matrix products  22.5 us (7%)
  between operations  14.4 us (5%)
    all_gather x1, waiting for transfers between devices, local(): lax.all_gather(gathered.astype(jnp.bfloat16), ('row', 'col'))  126 us
    ppermute x12, starting transfers between devices, extended(): lax.ppermute(lax.slice_in_dim(block, block.shape[dim] - width, None, axis...  57.3 us
    ppermute x12, starting transfers between devices, extended(): lax.ppermute(lax.slice_in_dim(block, 0, width, axis=dim), axis, backward)  15.5 us
    ppermute x12, waiting for transfers between devices, extended(): lax.ppermute(lax.slice_in_dim(block, 0, width, axis=dim), axis, backward)  13.2 us
    dot_general x36, matrix products, kernel_terms(): lax.dot_general(window, flat_signal, (((0,), (0,)), ((), ())), preferred_...  12.2 us
    conv_general_dilated x6, matrix products, convolve(): lax.conv_general_dilated(padded, kernel, (1, 1), 'VALID', dimension_numbe...  10.2 us
    ppermute x12, waiting for transfers between devices, extended(): lax.ppermute(lax.slice_in_dim(block, block.shape[dim] - width, None, axis...  7.71 us
  transfers between devices with their start and end apart: 27, of which 15 were waited for; matrix products, arithmetic and copies ran while one was open for 6% of the time, Pallas kernels for 0%

profile of v1, /device:TPU:0, one launch (start us, length us, event | category | flops | bytes accessed | tf_op | source)
XLA Modules:
  0.0 310.5 jit_solution(8141821143688731605)
XLA Ops:
  9.5 4.9 %collective-permute-start.9 = (bf16[4,1,32,128]{3,2,1,0:T(8,128)(2,1)S(1)}, bf16[4,1,32,128]{3,2,1,0:T(8,128)(2,1)S(1)}, u32[]{:S(2)}, u32[]{:S(2)}) collective-permute-start(bf16[4,1,32,128]{3,2,1,0:T(8,128)(2,1)S(1)} %get-tuple-element.397), channel_id=1, source_target_pairs={{0,4},{4,8},{8,12},{1,5},{5,9},{9,13},{2,6},{6,10},{10,14},{3,7},{... | collective-permute-start | bytes 98312 | tf_op jit(solution)/shard_map/ppermute | solution.py:12
  14.3 1.3 collective-permute-start.10
  16.0 4.2 %collective-permute-done.10 = bf16[4,1,32,128]{3,2,1,0:T(8,128)(2,1)S(1)} collective-permute-done((bf16[4,1,32,128]{3,2,1,0:T(8,128)(2,1)S(1)}, bf16[4,1,32,128]{3,2,1,0:T(8,128)(2,1)S(1)}, u32[]{:S(2)}, u32[]{:S(2)}) %collective-permute-start.10) | collective-permute-done | bytes 32800 | tf_op jit(solution)/shard_map/ppermute | solution.py:15
  20.8 3.5 %collective-permute-start.11 = (bf16[4,18,1,128]{3,2,1,0:T(2,128)(2,1)}, bf16[4,18,1,128]{3,2,1,0:T(2,128)(2,1)S(1)}, u32[]{:S(2)}, u32[]{:S(2)}) collective-permute-start(bf16[4,18,1,128]{3,2,1,0:T(2,128)(2,1)} %get-tuple-element.395), channel_id=1, source_target_pairs={{0,1},{1,2},{2,3},{4,5},{5,6},{6,7},{8,9},{9,10},{10,11},{12,13},{... | collective-permute-start | bytes 55304 | tf_op jit(solution)/shard_map/ppermute | solution.py:12
  24.3 1.3 collective-permute-start.12
  25.6 0.9 reverse_bitcast_fusion
  26.5 1.2 copy.112
  27.8 2.6 collective-permute-done.12
  32.0 1.7 fusion.39
  33.7 1.1 copy.103
  35.5 4.9 %collective-permute-start.13 = (bf16[4,1,32,128]{3,2,0,1:T(8,128)(2,1)}, bf16[4,1,32,128]{3,2,0,1:T(8,128)(2,1)}, u32[]{:S(2)}, u32[]{:S(2)}) collective-permute-start(bf16[4,1,32,128]{3,2,0,1:T(8,128)(2,1)} %slice_bitcast_fusion.5), channel_id=1, source_target_pairs={{0,4},{4,8},{8,12},{1,5},{5,9},{9,13},{2,6},{6,10},{10,14},{3,7},{... | collective-permute-start | bytes 98312 | tf_op jit(solution)/shard_map/ppermute | solution.py:12
  40.5 1.3 collective-permute-start.14
  41.8 1.1 slice_bitcast_fusion.3
  43.7 2.9 collective-permute-done.14
  46.7 3.5 %collective-permute-start.15 = (bf16[4,18,1,128]{3,1,2,0:T(8,128)(2,1)S(1)}, bf16[4,18,1,128]{3,1,2,0:T(8,128)(2,1)S(1)}, u32[]{:S(2)}, u32[]{:S(2)}) collective-permute-start(bf16[4,18,1,128]{3,1,2,0:T(8,128)(2,1)S(1)} %get-tuple-element.391), channel_id=1, source_target_pairs={{0,1},{1,2},{2,3},{4,5},{5,6},{6,7},{8,9},{9,10},{10,11},{12,13},{... | collective-permute-start | bytes 55304 | tf_op jit(solution)/shard_map/ppermute | solution.py:12
  50.2 1.3 collective-permute-start.16
  51.9 1.0 copy.113
  52.9 3.0 collective-permute-done.16
  55.9 1.4 pad_maximum_fusion.6
  58.9 1.7 fusion.38
  60.8 0.8 slice_bitcast_fusion.2
  61.7 0.9 broadcast.30.clone.1
  62.5 104.1 %while.20 = (s32[]{:T(128)}, bf16[4,16,32,128]{3,1,2,0:T(8,128)(2,1)}, bf16[4,16,32,128]{3,1,2,0:T(8,128)(2,1)}, f32[2,3,3,128,128]{3,4,2,1,0:T(8,128)S(1)}, pre...) while((s32[]{:T(128)}, ...), condition=%wide.region_1.2_spmd.clone, body=%wide.region_0.1_spmd.clone.sunk | while | flops 2737602560 | bytes 72510144 | solution.py:125
  62.5 1.7 multiply_convert_fusion.2
  64.3 1.3 collective-permute-start
  65.6 4.5 %collective-permute-start.1 = (bf16[4,1,32,128]{3,1,2,0:T(2,128)(2,1)S(1)}, bf16[4,1,32,128]{3,1,2,0:T(2,128)(2,1)S(1)}, u32[]{:S(2)}, u32[]{:S(2)}) collective-permute-start(bf16[4,1,32,128]{3,1,2,0:T(2,128)(2,1)S(1)} %get-tuple-element.485), channel_id=1, source_target_pairs={{0,4},{4,8},{8,12},{1,5},{5,9},{9,13},{2,6},{6,10},{10,14},{3,7},{... | collective-permute-start | bytes 98312 | tf_op jit(solution)/shard_map/while/body/eval_jaxpr/ppermute | solution.py:12
  73.4 1.3 collective-permute-start.2
  74.7 5.2 %collective-permute-start.3 = (bf16[4,18,1,128]{3,1,2,0:T(8,128)(2,1)S(1)}, bf16[4,18,1,128]{3,1,2,0:T(8,128)(2,1)}, u32[]{:S(2)}, u32[]{:S(2)}) collective-permute-start(bf16[4,18,1,128]{3,1,2,0:T(8,128)(2,1)S(1)} %get-tuple-element.487), channel_id=1, source_target_pairs={{0,1},{1,2},{2,3},{4,5},{5,6},{6,7},{8,9},{9,10},{10,11},{12,13},{... | collective-permute-start | bytes 55304 | tf_op jit(solution)/shard_map/while/body/eval_jaxpr/ppermute | solution.py:12
  80.0 0.8 collective-permute-done.3
  80.8 1.2 maximum_bitcast_fusion.18
  83.6 1.7 convolution_select_fusion.5
  86.2 1.0 copy-done.5
  90.4 1.3 collective-permute-start.4
  91.7 4.5 %collective-permute-start.5 = (bf16[4,1,32,128]{3,1,2,0:T(2,128)(2,1)S(1)}, bf16[4,1,32,128]{3,1,2,0:T(2,128)(2,1)S(1)}, u32[]{:S(2)}, u32[]{:S(2)}) collective-permute-start(bf16[4,1,32,128]{3,1,2,0:T(2,128)(2,1)S(1)} %get-tuple-element.489), channel_id=1, source_target_pairs={{0,4},{4,8},{8,12},{1,5},{5,9},{9,13},{2,6},{6,10},{10,14},{3,7},{... | collective-permute-start | bytes 98312 | tf_op jit(solution)/shard_map/while/body/eval_jaxpr/ppermute | solution.py:12
  96.6 1.6 collective-permute-done.5
  98.2 1.3 collective-permute-start.6
  99.5 4.9 %collective-permute-start.7 = (bf16[4,18,1,128]{3,1,2,0:T(8,128)(2,1)S(1)}, bf16[4,18,1,128]{3,1,2,0:T(8,128)(2,1)S(1)}, u32[]{:S(2)}, u32[]{:S(2)}) collective-permute-start(bf16[4,18,1,128]{3,1,2,0:T(8,128)(2,1)S(1)} %get-tuple-element.491), channel_id=1, source_target_pairs={{0,1},{1,2},{2,3},{4,5},{5,6},{6,7},{8,9},{9,10},{10,11},{12,13},{... | collective-permute-start | bytes 55304 | tf_op jit(solution)/shard_map/while/body/eval_jaxpr/ppermute | solution.py:12
  104.5 1.4 collective-permute-done.7
  107.5 1.7 fusion.166
  109.5 1.3 collective-permute-start.8
  111.2 0.9 select_select_fusion.2
  112.1 1.3 collective-permute-done.8
  113.4 1.7 multiply_convert_fusion.2
  115.3 1.3 collective-permute-start
  116.6 5.2 %collective-permute-start.1 = (bf16[4,1,32,128]{3,1,2,0:T(2,128)(2,1)S(1)}, bf16[4,1,32,128]{3,1,2,0:T(2,128)(2,1)S(1)}, u32[]{:S(2)}, u32[]{:S(2)}) collective-permute-start(bf16[4,1,32,128]{3,1,2,0:T(2,128)(2,1)S(1)} %get-tuple-element.485), channel_id=1, source_target_pairs={{0,4},{4,8},{8,12},{1,5},{5,9},{9,13},{2,6},{6,10},{10,14},{3,7},{... | collective-permute-start | bytes 98312 | tf_op jit(solution)/shard_map/while/body/eval_jaxpr/ppermute | solution.py:12
  125.0 1.3 collective-permute-start.2
  126.3 5.4 %collective-permute-start.3 = (bf16[4,18,1,128]{3,1,2,0:T(8,128)(2,1)S(1)}, bf16[4,18,1,128]{3,1,2,0:T(8,128)(2,1)}, u32[]{:S(2)}, u32[]{:S(2)}) collective-permute-start(bf16[4,18,1,128]{3,1,2,0:T(8,128)(2,1)S(1)} %get-tuple-element.487), channel_id=1, source_target_pairs={{0,1},{1,2},{2,3},{4,5},{5,6},{6,7},{8,9},{9,10},{10,11},{12,13},{... | collective-permute-start | bytes 55304 | tf_op jit(solution)/shard_map/while/body/eval_jaxpr/ppermute | solution.py:12
  132.7 1.2 maximum_bitcast_fusion.18
  135.5 1.7 convolution_select_fusion.5
  138.1 1.0 copy-done.5
  142.3 1.3 collective-permute-start.4
  143.6 5.8 %collective-permute-start.5 = (bf16[4,1,32,128]{3,1,2,0:T(2,128)(2,1)S(1)}, bf16[4,1,32,128]{3,1,2,0:T(2,128)(2,1)S(1)}, u32[]{:S(2)}, u32[]{:S(2)}) collective-permute-start(bf16[4,1,32,128]{3,1,2,0:T(2,128)(2,1)S(1)} %get-tuple-element.489), channel_id=1, source_target_pairs={{0,4},{4,8},{8,12},{1,5},{5,9},{9,13},{2,6},{6,10},{10,14},{3,7},{... | collective-permute-start | bytes 98312 | tf_op jit(solution)/shard_map/while/body/eval_jaxpr/ppermute | solution.py:12
  149.7 1.6 collective-permute-done.5
  151.3 1.3 collective-permute-start.6
  152.6 4.9 %collective-permute-start.7 = (bf16[4,18,1,128]{3,1,2,0:T(8,128)(2,1)S(1)}, bf16[4,18,1,128]{3,1,2,0:T(8,128)(2,1)S(1)}, u32[]{:S(2)}, u32[]{:S(2)}) collective-permute-start(bf16[4,18,1,128]{3,1,2,0:T(8,128)(2,1)S(1)} %get-tuple-element.491), channel_id=1, source_target_pairs={{0,1},{1,2},{2,3},{4,5},{5,6},{6,7},{8,9},{9,10},{10,11},{12,13},{... | collective-permute-start | bytes 55304 | tf_op jit(solution)/shard_map/while/body/eval_jaxpr/ppermute | solution.py:12
  157.6 1.4 collective-permute-done.7
  160.6 1.7 fusion.166
  162.6 1.3 collective-permute-start.8
  164.3 2.0 select_select_fusion.2
  166.6 1.1 copy.115
  167.7 1.2 copy.114
  169.7 126.2 %all-gather.3.cloned.1.call-done = bf16[32,3,3,128,128]{4,3,2,1,0:T(8,128)(2,1)} async-done(((bf16[2,3,3,128,128]{4,3,2,1,0:T(8,128)(2,1)}), bf16[32,3,3,128,128]{4,3,2,1,0:T(8,128)(2,1)}) %all-gather.3.cloned.1.call-update) | async-done | bytes 9437200 | tf_op jit(solution)/shard_map/all_gather | solution.py:129
  296.0 5.8 %reduce_sum.12 = bf16[2,3,3,128,128]{4,3,2,1,0:T(8,128)(2,1)S(1)} reduce(bf16[16,2,3,3,128,128]{5,4,3,2,1,0:T(8,128)(2,1)} %bitcast.360, bf16[]{:T(256)} %constant.67.clone.1), dimensions={0}, to_apply=%region_3.4 | reduce | flops 4423680 | bytes 10027010 | tf_op jit(solution)/shard_map/reduce_sum | solution.py:129
  302.2 1.4 copy.117
  (169 shorter events, 34.0 us)
Async XLA Ops:
  7.2 1.5 copy-start
  7.2 8.5 %copy-start.6 = (bf16[2,3,3,128,128]{4,3,2,1,0:T(8,128)(2,1)S(1)}, bf16[2,3,3,128,128]{4,3,2,1,0:T(8,128)(2,1)}, u32[]{:S(2)}) copy-start(bf16[2,3,3,128,128]{4,3,2,1,0:T(8,128)(2,1)} %param.7) | copy-start | bytes 1769476
  7.2 288.8 %all-gather.3.cloned.1.call-start = ((), (), s32[]{:S(2)}) async-start(), calls=%async_computation | async-start | bytes 10027008 | tf_op jit(solution)/shard_map/all_gather | solution.py:129
  8.0 0.7 copy-start.9
  9.5 6.5 %collective-permute-start.9 = (bf16[4,1,32,128]{3,2,1,0:T(8,128)(2,1)S(1)}, bf16[4,1,32,128]{3,2,1,0:T(8,128)(2,1)S(1)}, u32[]{:S(2)}, u32[]{:S(2)}) collective-permute-start(bf16[4,1,32,128]{3,2,1,0:T(8,128)(2,1)S(1)} %get-tuple-element.397), channel_id=1, source_target_pairs={{0,4},{4,8},{8,12},{1,5},{5,9},{9,13},{2,6},{6,10},{10,14},{3,7},{... | collective-permute-start | bytes 98312 | tf_op jit(solution)/shard_map/ppermute | solution.py:12
  14.3 5.8 %collective-permute-start.10 = (bf16[4,1,32,128]{3,2,1,0:T(8,128)(2,1)S(1)}, bf16[4,1,32,128]{3,2,1,0:T(8,128)(2,1)S(1)}, u32[]{:S(2)}, u32[]{:S(2)}) collective-permute-start(bf16[4,1,32,128]{3,2,1,0:T(8,128)(2,1)S(1)} %get-tuple-element.398), channel_id=1, source_target_pairs={{4,0},{8,4},{12,8},{5,1},{9,5},{13,9},{6,2},{10,6},{14,10},{7,3},{... | collective-permute-start | bytes 98312 | tf_op jit(solution)/shard_map/ppermute | solution.py:15
  20.8 6.9 %collective-permute-start.11 = (bf16[4,18,1,128]{3,2,1,0:T(2,128)(2,1)}, bf16[4,18,1,128]{3,2,1,0:T(2,128)(2,1)S(1)}, u32[]{:S(2)}, u32[]{:S(2)}) collective-permute-start(bf16[4,18,1,128]{3,2,1,0:T(2,128)(2,1)} %get-tuple-element.395), channel_id=1, source_target_pairs={{0,1},{1,2},{2,3},{4,5},{5,6},{6,7},{8,9},{9,10},{10,11},{12,13},{... | collective-permute-start | bytes 55304 | tf_op jit(solution)/shard_map/ppermute | solution.py:12
  24.3 6.1 %collective-permute-start.12 = (bf16[4,18,1,128]{3,2,1,0:T(2,128)(2,1)}, bf16[4,18,1,128]{3,2,1,0:T(2,128)(2,1)S(1)}, u32[]{:S(2)}, u32[]{:S(2)}) collective-permute-start(bf16[4,18,1,128]{3,2,1,0:T(2,128)(2,1)} %get-tuple-element.396), channel_id=1, source_target_pairs={{1,0},{2,1},{3,2},{5,4},{6,5},{7,6},{9,8},{10,9},{11,10},{13,12},{... | collective-permute-start | bytes 55304 | tf_op jit(solution)/shard_map/ppermute | solution.py:15
  31.3 0.7 copy-start.11
  35.5 7.4 %collective-permute-start.13 = (bf16[4,1,32,128]{3,2,0,1:T(8,128)(2,1)}, bf16[4,1,32,128]{3,2,0,1:T(8,128)(2,1)}, u32[]{:S(2)}, u32[]{:S(2)}) collective-permute-start(bf16[4,1,32,128]{3,2,0,1:T(8,128)(2,1)} %slice_bitcast_fusion.5), channel_id=1, source_target_pairs={{0,4},{4,8},{8,12},{1,5},{5,9},{9,13},{2,6},{6,10},{10,14},{3,7},{... | collective-permute-start | bytes 98312 | tf_op jit(solution)/shard_map/ppermute | solution.py:12
  40.5 6.2 %collective-permute-start.14 = (bf16[4,1,32,128]{3,1,2,0:T(2,128)(2,1)S(1)}, bf16[4,1,32,128]{3,1,2,0:T(2,128)(2,1)S(1)}, u32[]{:S(2)}, u32[]{:S(2)}) collective-permute-start(bf16[4,1,32,128]{3,1,2,0:T(2,128)(2,1)S(1)} %copy.105), channel_id=1, source_target_pairs={{4,0},{8,4},{12,8},{5,1},{9,5},{13,9},{6,2},{10,6},{14,10},{7,3},{... | collective-permute-start | bytes 98312 | tf_op jit(solution)/shard_map/ppermute | solution.py:15
  46.7 6.3 %collective-permute-start.15 = (bf16[4,18,1,128]{3,1,2,0:T(8,128)(2,1)S(1)}, bf16[4,18,1,128]{3,1,2,0:T(8,128)(2,1)S(1)}, u32[]{:S(2)}, u32[]{:S(2)}) collective-permute-start(bf16[4,18,1,128]{3,1,2,0:T(8,128)(2,1)S(1)} %get-tuple-element.391), channel_id=1, source_target_pairs={{0,1},{1,2},{2,3},{4,5},{5,6},{6,7},{8,9},{9,10},{10,11},{12,13},{... | collective-permute-start | bytes 55304 | tf_op jit(solution)/shard_map/ppermute | solution.py:12
  50.2 5.7 %collective-permute-start.16 = (bf16[4,18,1,128]{3,1,2,0:T(8,128)(2,1)S(1)}, bf16[4,18,1,128]{3,1,2,0:T(8,128)(2,1)S(1)}, u32[]{:S(2)}, u32[]{:S(2)}) collective-permute-start(bf16[4,18,1,128]{3,1,2,0:T(8,128)(2,1)S(1)} %get-tuple-element.392), channel_id=1, source_target_pairs={{1,0},{2,1},{3,2},{5,4},{6,5},{7,6},{9,8},{10,9},{11,10},{13,12},{... | collective-permute-start | bytes 55304 | tf_op jit(solution)/shard_map/ppermute | solution.py:15
  57.8 1.1 copy-start.7
  62.5 8.0 %copy-start.1 = (bf16[4,16,32,128]{3,1,2,0:T(8,128)(2,1)}, bf16[4,16,32,128]{3,1,2,0:T(8,128)(2,1)S(1)}, u32[]{:S(2)}) copy-start(bf16[4,16,32,128]{3,1,2,0:T(8,128)(2,1)S(1)} %get-tuple-element.533) | copy-start | bytes 1572868 | tf_op jit(solution)/shard_map/while
  62.5 7.7 %copy-start.4 = (bf16[4,18,34,128]{3,1,2,0:T(8,128)(2,1)S(1)}, bf16[4,18,34,128]{3,1,2,0:T(8,128)(2,1)}, u32[]{:S(2)}) copy-start(bf16[4,18,34,128]{3,1,2,0:T(8,128)(2,1)} %get-tuple-element.539) | copy-start | bytes 1880068 | tf_op jit(solution)/shard_map/while
  64.3 9.0 %collective-permute-start = (bf16[4,1,32,128]{3,1,2,0:T(2,128)(2,1)S(1)}, bf16[4,1,32,128]{3,1,2,0:T(2,128)(2,1)S(1)}, u32[]{:S(2)}, u32[]{:S(2)}) collective-permute-start(bf16[4,1,32,128]{3,1,2,0:T(2,128)(2,1)S(1)} %get-tuple-element.484), channel_id=1, source_target_pairs={{4,0},{8,4},{12,8},{5,1},{9,5},{13,9},{6,2},{10,6},{14,10},{7,3},{... | collective-permute-start | bytes 98312 | tf_op jit(solution)/shard_map/while/body/eval_jaxpr/ppermute | solution.py:15
  65.6 7.8 %collective-permute-start.1 = (bf16[4,1,32,128]{3,1,2,0:T(2,128)(2,1)S(1)}, bf16[4,1,32,128]{3,1,2,0:T(2,128)(2,1)S(1)}, u32[]{:S(2)}, u32[]{:S(2)}) collective-permute-start(bf16[4,1,32,128]{3,1,2,0:T(2,128)(2,1)S(1)} %get-tuple-element.485), channel_id=1, source_target_pairs={{0,4},{4,8},{8,12},{1,5},{5,9},{9,13},{2,6},{6,10},{10,14},{3,7},{... | collective-permute-start | bytes 98312 | tf_op jit(solution)/shard_map/while/body/eval_jaxpr/ppermute | solution.py:12
  73.4 6.5 %collective-permute-start.2 = (bf16[4,18,1,128]{3,1,2,0:T(8,128)(2,1)S(1)}, bf16[4,18,1,128]{3,1,2,0:T(8,128)(2,1)S(1)}, u32[]{:S(2)}, u32[]{:S(2)}) collective-permute-start(bf16[4,18,1,128]{3,1,2,0:T(8,128)(2,1)S(1)} %get-tuple-element.486), channel_id=1, source_target_pairs={{1,0},{2,1},{3,2},{5,4},{6,5},{7,6},{9,8},{10,9},{11,10},{13,12},{... | collective-permute-start | bytes 55304 | tf_op jit(solution)/shard_map/while/body/eval_jaxpr/ppermute | solution.py:15
  74.7 6.1 %collective-permute-start.3 = (bf16[4,18,1,128]{3,1,2,0:T(8,128)(2,1)S(1)}, bf16[4,18,1,128]{3,1,2,0:T(8,128)(2,1)}, u32[]{:S(2)}, u32[]{:S(2)}) collective-permute-start(bf16[4,18,1,128]{3,1,2,0:T(8,128)(2,1)S(1)} %get-tuple-element.487), channel_id=1, source_target_pairs={{0,1},{1,2},{2,3},{4,5},{5,6},{6,7},{8,9},{9,10},{10,11},{12,13},{... | collective-permute-start | bytes 55304 | tf_op jit(solution)/shard_map/while/body/eval_jaxpr/ppermute | solution.py:12
  82.5 1.1 copy-start.8
  86.1 1.2 copy-start.5
  90.4 6.2 %collective-permute-start.4 = (bf16[4,1,32,128]{3,1,2,0:T(2,128)(2,1)S(1)}, bf16[4,1,32,128]{3,1,2,0:T(2,128)(2,1)S(1)}, u32[]{:S(2)}, u32[]{:S(2)}) collective-permute-start(bf16[4,1,32,128]{3,1,2,0:T(2,128)(2,1)S(1)} %get-tuple-element.488), channel_id=1, source_target_pairs={{4,0},{8,4},{12,8},{5,1},{9,5},{13,9},{6,2},{10,6},{14,10},{7,3},{... | collective-permute-start | bytes 98312 | tf_op jit(solution)/shard_map/while/body/eval_jaxpr/ppermute | solution.py:15
  91.7 6.4 %collective-permute-start.5 = (bf16[4,1,32,128]{3,1,2,0:T(2,128)(2,1)S(1)}, bf16[4,1,32,128]{3,1,2,0:T(2,128)(2,1)S(1)}, u32[]{:S(2)}, u32[]{:S(2)}) collective-permute-start(bf16[4,1,32,128]{3,1,2,0:T(2,128)(2,1)S(1)} %get-tuple-element.489), channel_id=1, source_target_pairs={{0,4},{4,8},{8,12},{1,5},{5,9},{9,13},{2,6},{6,10},{10,14},{3,7},{... | collective-permute-start | bytes 98312 | tf_op jit(solution)/shard_map/while/body/eval_jaxpr/ppermute | solution.py:12
  98.2 6.3 %collective-permute-start.6 = (bf16[4,18,1,128]{3,1,2,0:T(8,128)(2,1)S(1)}, bf16[4,18,1,128]{3,1,2,0:T(8,128)(2,1)S(1)}, u32[]{:S(2)}, u32[]{:S(2)}) collective-permute-start(bf16[4,18,1,128]{3,1,2,0:T(8,128)(2,1)S(1)} %get-tuple-element.490), channel_id=1, source_target_pairs={{1,0},{2,1},{3,2},{5,4},{6,5},{7,6},{9,8},{10,9},{11,10},{13,12},{... | collective-permute-start | bytes 55304 | tf_op jit(solution)/shard_map/while/body/eval_jaxpr/ppermute | solution.py:15
  99.5 6.5 %collective-permute-start.7 = (bf16[4,18,1,128]{3,1,2,0:T(8,128)(2,1)S(1)}, bf16[4,18,1,128]{3,1,2,0:T(8,128)(2,1)S(1)}, u32[]{:S(2)}, u32[]{:S(2)}) collective-permute-start(bf16[4,18,1,128]{3,1,2,0:T(8,128)(2,1)S(1)} %get-tuple-element.491), channel_id=1, source_target_pairs={{0,1},{1,2},{2,3},{4,5},{5,6},{6,7},{8,9},{9,10},{10,11},{12,13},{... | collective-permute-start | bytes 55304 | tf_op jit(solution)/shard_map/while/body/eval_jaxpr/ppermute | solution.py:12
  109.5 3.9 %collective-permute-start.8 = (bf16[4,16,32,128]{3,1,2,0:T(8,128)(2,1)S(1)}, bf16[4,16,32,128]{3,1,2,0:T(8,128)(2,1)}, u32[]{:S(2)}, u32[]{:S(2)}) collective-permute-start(bf16[4,16,32,128]{3,1,2,0:T(8,128)(2,1)S(1)} %slice_bitcast_fusion.7), channel_id=1, source_target_pairs={{16,0},{17,1},{18,2},{19,3},{20,4},{21,5},{22,6},{23,7},{24,8},{25... | collective-permute-start | bytes 1572872 | tf_op jit(solution)/shard_map/while/body/eval_jaxpr/ppermute | solution.py:23
  111.2 2.2 copy-start.2
  113.4 8.7 %copy-start.1 = (bf16[4,16,32,128]{3,1,2,0:T(8,128)(2,1)}, bf16[4,16,32,128]{3,1,2,0:T(8,128)(2,1)S(1)}, u32[]{:S(2)}) copy-start(bf16[4,16,32,128]{3,1,2,0:T(8,128)(2,1)S(1)} %get-tuple-element.533) | copy-start | bytes 1572868 | tf_op jit(solution)/shard_map/while
  113.4 8.4 %copy-start.4 = (bf16[4,18,34,128]{3,1,2,0:T(8,128)(2,1)S(1)}, bf16[4,18,34,128]{3,1,2,0:T(8,128)(2,1)}, u32[]{:S(2)}) copy-start(bf16[4,18,34,128]{3,1,2,0:T(8,128)(2,1)} %get-tuple-element.539) | copy-start | bytes 1880068 | tf_op jit(solution)/shard_map/while
  115.3 9.7 %collective-permute-start = (bf16[4,1,32,128]{3,1,2,0:T(2,128)(2,1)S(1)}, bf16[4,1,32,128]{3,1,2,0:T(2,128)(2,1)S(1)}, u32[]{:S(2)}, u32[]{:S(2)}) collective-permute-start(bf16[4,1,32,128]{3,1,2,0:T(2,128)(2,1)S(1)} %get-tuple-element.484), channel_id=1, source_target_pairs={{4,0},{8,4},{12,8},{5,1},{9,5},{13,9},{6,2},{10,6},{14,10},{7,3},{... | collective-permute-start | bytes 98312 | tf_op jit(solution)/shard_map/while/body/eval_jaxpr/ppermute | solution.py:15
  116.6 8.4 %collective-permute-start.1 = (bf16[4,1,32,128]{3,1,2,0:T(2,128)(2,1)S(1)}, bf16[4,1,32,128]{3,1,2,0:T(2,128)(2,1)S(1)}, u32[]{:S(2)}, u32[]{:S(2)}) collective-permute-start(bf16[4,1,32,128]{3,1,2,0:T(2,128)(2,1)S(1)} %get-tuple-element.485), channel_id=1, source_target_pairs={{0,4},{4,8},{8,12},{1,5},{5,9},{9,13},{2,6},{6,10},{10,14},{3,7},{... | collective-permute-start | bytes 98312 | tf_op jit(solution)/shard_map/while/body/eval_jaxpr/ppermute | solution.py:12
  125.0 6.8 %collective-permute-start.2 = (bf16[4,18,1,128]{3,1,2,0:T(8,128)(2,1)S(1)}, bf16[4,18,1,128]{3,1,2,0:T(8,128)(2,1)S(1)}, u32[]{:S(2)}, u32[]{:S(2)}) collective-permute-start(bf16[4,18,1,128]{3,1,2,0:T(8,128)(2,1)S(1)} %get-tuple-element.486), channel_id=1, source_target_pairs={{1,0},{2,1},{3,2},{5,4},{6,5},{7,6},{9,8},{10,9},{11,10},{13,12},{... | collective-permute-start | bytes 55304 | tf_op jit(solution)/shard_map/while/body/eval_jaxpr/ppermute | solution.py:15
  126.3 6.3 %collective-permute-start.3 = (bf16[4,18,1,128]{3,1,2,0:T(8,128)(2,1)S(1)}, bf16[4,18,1,128]{3,1,2,0:T(8,128)(2,1)}, u32[]{:S(2)}, u32[]{:S(2)}) collective-permute-start(bf16[4,18,1,128]{3,1,2,0:T(8,128)(2,1)S(1)} %get-tuple-element.487), channel_id=1, source_target_pairs={{0,1},{1,2},{2,3},{4,5},{5,6},{6,7},{8,9},{9,10},{10,11},{12,13},{... | collective-permute-start | bytes 55304 | tf_op jit(solution)/shard_map/while/body/eval_jaxpr/ppermute | solution.py:12
  134.4 1.1 copy-start.8
  138.0 1.2 copy-start.5
  142.3 7.4 %collective-permute-start.4 = (bf16[4,1,32,128]{3,1,2,0:T(2,128)(2,1)S(1)}, bf16[4,1,32,128]{3,1,2,0:T(2,128)(2,1)S(1)}, u32[]{:S(2)}, u32[]{:S(2)}) collective-permute-start(bf16[4,1,32,128]{3,1,2,0:T(2,128)(2,1)S(1)} %get-tuple-element.488), channel_id=1, source_target_pairs={{4,0},{8,4},{12,8},{5,1},{9,5},{13,9},{6,2},{10,6},{14,10},{7,3},{... | collective-permute-start | bytes 98312 | tf_op jit(solution)/shard_map/while/body/eval_jaxpr/ppermute | solution.py:15
  143.6 7.7 %collective-permute-start.5 = (bf16[4,1,32,128]{3,1,2,0:T(2,128)(2,1)S(1)}, bf16[4,1,32,128]{3,1,2,0:T(2,128)(2,1)S(1)}, u32[]{:S(2)}, u32[]{:S(2)}) collective-permute-start(bf16[4,1,32,128]{3,1,2,0:T(2,128)(2,1)S(1)} %get-tuple-element.489), channel_id=1, source_target_pairs={{0,4},{4,8},{8,12},{1,5},{5,9},{9,13},{2,6},{6,10},{10,14},{3,7},{... | collective-permute-start | bytes 98312 | tf_op jit(solution)/shard_map/while/body/eval_jaxpr/ppermute | solution.py:12
  151.3 6.3 %collective-permute-start.6 = (bf16[4,18,1,128]{3,1,2,0:T(8,128)(2,1)S(1)}, bf16[4,18,1,128]{3,1,2,0:T(8,128)(2,1)S(1)}, u32[]{:S(2)}, u32[]{:S(2)}) collective-permute-start(bf16[4,18,1,128]{3,1,2,0:T(8,128)(2,1)S(1)} %get-tuple-element.490), channel_id=1, source_target_pairs={{1,0},{2,1},{3,2},{5,4},{6,5},{7,6},{9,8},{10,9},{11,10},{13,12},{... | collective-permute-start | bytes 55304 | tf_op jit(solution)/shard_map/while/body/eval_jaxpr/ppermute | solution.py:15
  152.6 6.5 %collective-permute-start.7 = (bf16[4,18,1,128]{3,1,2,0:T(8,128)(2,1)S(1)}, bf16[4,18,1,128]{3,1,2,0:T(8,128)(2,1)S(1)}, u32[]{:S(2)}, u32[]{:S(2)}) collective-permute-start(bf16[4,18,1,128]{3,1,2,0:T(8,128)(2,1)S(1)} %get-tuple-element.491), channel_id=1, source_target_pairs={{0,1},{1,2},{2,3},{4,5},{5,6},{6,7},{8,9},{9,10},{10,11},{12,13},{... | collective-permute-start | bytes 55304 | tf_op jit(solution)/shard_map/while/body/eval_jaxpr/ppermute | solution.py:12
  162.6 3.9 %collective-permute-start.8 = (bf16[4,16,32,128]{3,1,2,0:T(8,128)(2,1)S(1)}, bf16[4,16,32,128]{3,1,2,0:T(8,128)(2,1)}, u32[]{:S(2)}, u32[]{:S(2)}) collective-permute-start(bf16[4,16,32,128]{3,1,2,0:T(8,128)(2,1)S(1)} %slice_bitcast_fusion.7), channel_id=1, source_target_pairs={{16,0},{17,1},{18,2},{19,3},{20,4},{21,5},{22,6},{23,7},{24,8},{25... | collective-permute-start | bytes 1572872 | tf_op jit(solution)/shard_map/while/body/eval_jaxpr/ppermute | solution.py:23
  164.3 2.2 copy-start.2
  167.6 1.3 copy-start.10
  169.7 132.1 %copy-start.3 = (bf16[4,16,32,128]{3,2,1,0:T(8,128)(2,1)}, bf16[4,16,32,128]{3,2,1,0:T(8,128)(2,1)S(1)}, u32[]{:S(2)}) copy-start(bf16[4,16,32,128]{3,2,1,0:T(8,128)(2,1)S(1)} %scatter_fusion) | copy-start | bytes 1572868
Sparse Core Ops, SparseCore 0:
  167.8 128.1 all-gather.2
